TPU v7x, 256 devices: a whole 4x4x8 slice. The times are simulated.
256 devices in a mesh: win: 32 (over y, z), grp: 8 (over x, core).
Axes of the slice: x: 4, y: 4, z: 8, core: 2. Of those that a mesh axis runs over, the one named last changes fastest.
Arguments:
- points: bfloat16 [32, 8, 512, 512], P('win', 'grp'), may hold values from -6 to 6
- rank: int32 [32, 8, 512], P('win', 'grp'), may hold values from 0 to 16383, as said below
- counts: int32 [8, 32, 8], replicated, may hold values from 1 to 128, 512 in all within a row
- w_qkv_one: bfloat16 [512, 1536], replicated
- w_out_one: bfloat16 [512, 512], replicated, may hold values from -0.25 to 0.25
- w_up: bfloat16 [512, 2048], replicated, may hold values from -0.25 to 0.25
- w_down: bfloat16 [2048, 512], replicated, may hold values from -0.125 to 0.125
- w_qkv_two: bfloat16 [512, 1536], replicated
- w_out_two: bfloat16 [512, 512], replicated, may hold values from -0.25 to 0.25
Outputs:
- encoded: bfloat16 [32, 8, 512, 512], P('win', 'grp')
Inputs may be any that keep to these rules, and one draw needn't show every extreme that they name: Within each of the 8 grp columns, rank over all 32 devices of win is a permutation of 0 to 16383. Each device holds at most 32 points whose rank // 512 is any one owner, and exactly 32 for some owner; each owner receives exactly 32 from some device. For each grp column and owner the 8 counts sum to 512, and the largest is 128.
All inputs are finite; a program needn't handle non-finite values.
Results may differ from a plain program's by a relative error of at most 0.03.
The roundings to bfloat16 on the way count: a program that leaves them out, or rounds other values in their place, can miss the bound.
Values may be sent and summed in bfloat16 or wider, within the bound.
No kernel may reach another device: no remote copies, remote signals or barrier semaphores. Data moves between devices by JAX's collectives and lax.ppermute only.
A program may use at most 128 MiB of HBM per device.

v0:
```python
import jax
import jax.numpy as jnp
from jax import lax
from jax.sharding import PartitionSpec as P

HEAD_DIM = 32
WINDOW_SLOTS = 128
EPSILON = 1e-05
MASKED = -1e30


def normalize(row_data):
    values = row_data.astype(jnp.float32)
    center = values - jnp.mean(values, axis=-1, keepdims=True)
    spread = jnp.mean(center * center, axis=-1, keepdims=True)
    return (center * lax.rsqrt(spread + EPSILON)).astype(jnp.bfloat16)


def project(row_data, weight):
    return jnp.dot(normalize(row_data), weight, preferred_element_type=jnp.float32).astype(
        jnp.bfloat16
    )


def attention_core(packed, valid):
    block_count, width_len, triple = packed.shape
    model_dim = triple // 3
    heads_count = model_dim // HEAD_DIM
    split_heads = packed.reshape(block_count, width_len, 3, heads_count, HEAD_DIM)
    scores = jnp.einsum(
        "bqhe,bkhe->bhqk",
        split_heads[:, :, 0],
        split_heads[:, :, 1],
        preferred_element_type=jnp.float32,
    ) * HEAD_DIM ** (-0.5)
    scores = jnp.where(valid[:, None, None, :], scores, MASKED)
    row_max = jnp.max(scores, axis=-1, keepdims=True)
    weights = jnp.exp(scores - row_max)
    weights = (weights / jnp.sum(weights, axis=-1, keepdims=True)).astype(jnp.bfloat16)
    context = jnp.einsum(
        "bhqk,bkhe->bqhe", weights, split_heads[:, :, 2], preferred_element_type=jnp.float32
    )
    return context.astype(jnp.bfloat16).reshape(block_count * width_len, model_dim)


def residual_add(row_data, context, weight):
    return (
        row_data.astype(jnp.float32) + jnp.dot(context, weight, preferred_element_type=jnp.float32)
    ).astype(jnp.bfloat16)


def feed_forward(row_data, w_up, w_down):
    hidden = jax.nn.gelu(
        jnp.dot(normalize(row_data), w_up, preferred_element_type=jnp.float32), approximate=True
    ).astype(jnp.bfloat16)
    return (
        row_data.astype(jnp.float32) + jnp.dot(hidden, w_down, preferred_element_type=jnp.float32)
    ).astype(jnp.bfloat16)


def on_device(points, rank, counts, w_qkv_one, w_out_one, w_up, w_down, w_qkv_two, w_out_two):
    owner_count = lax.axis_size("win")
    group_count = lax.axis_size("grp")
    win_index = lax.axis_index("win")
    grp_index = lax.axis_index("grp")
    local_points = points.shape[2]
    model_dim = points.shape[3]
    blocks = counts.shape[2]
    slots_all = blocks * WINDOW_SLOTS
    capacity = 2 * local_points // owner_count
    dilation_stride = WINDOW_SLOTS // group_count
    rows_x = points.reshape(local_points, model_dim)
    point_rank = rank.reshape(local_points)
    block_ids = jnp.arange(blocks, dtype=jnp.int32)
    column_counts = lax.dynamic_index_in_dim(counts, grp_index, 0, keepdims=False)
    window_ends = jnp.cumsum(column_counts, axis=1)
    starts = window_ends - column_counts
    owner_dev = point_rank // local_points
    offset = point_rank % local_points
    choose = (owner_dev[:, None] == jnp.arange(owner_count, dtype=jnp.int32)[None, :]).astype(
        jnp.int32
    )
    owner_ends = jnp.sum(choose[:, :, None] * window_ends[None], axis=1)
    owner_starts = jnp.sum(choose[:, :, None] * starts[None], axis=1)
    window = jnp.sum((owner_ends <= offset[:, None]).astype(jnp.int32), axis=1)
    block_pick = (window[:, None] == block_ids[None, :]).astype(jnp.int32)
    dest_slot = window * WINDOW_SLOTS + offset - jnp.sum(block_pick * owner_starts, axis=1)
    peer_order = jnp.sum(choose * (jnp.cumsum(choose, axis=0) - 1), axis=1)
    send_place = owner_dev * capacity + peer_order
    outgoing = (
        jnp.zeros((owner_count * capacity, model_dim), jnp.bfloat16).at[send_place].set(rows_x)
    )
    outgoing_slot = (
        jnp.full((owner_count * capacity,), slots_all, jnp.int32).at[send_place].set(dest_slot)
    )
    arrived, arrived_slot = (
        lax.all_to_all(outgoing, "win", split_axis=0, concat_axis=0, tiled=True),
        lax.all_to_all(outgoing_slot, "win", split_axis=0, concat_axis=0, tiled=True),
    )
    own_counts = lax.dynamic_index_in_dim(column_counts, win_index, 0, keepdims=False)
    column = jnp.arange(WINDOW_SLOTS, dtype=jnp.int32)
    usable_mask = column[None, :] < own_counts[:, None]
    padded_x = (
        jnp.zeros((slots_all, model_dim), jnp.bfloat16).at[arrived_slot].set(arrived, mode="drop")
    )
    packed = project(padded_x, w_qkv_one).reshape(blocks, WINDOW_SLOTS, 3 * model_dim)
    context = attention_core(packed, usable_mask)
    first_pad = feed_forward(residual_add(padded_x, context, w_out_one), w_up, w_down)
    mask_send = usable_mask.astype(jnp.bfloat16).reshape(blocks, dilation_stride, group_count)
    dilated_rows = lax.all_to_all(
        first_pad.reshape(blocks, dilation_stride, group_count, model_dim),
        "grp",
        split_axis=2,
        concat_axis=1,
        tiled=True,
    )
    valid_marks = lax.all_to_all(mask_send, "grp", split_axis=2, concat_axis=1, tiled=True)
    block_count = dilated_rows.shape[0]
    flat_rows = dilated_rows.reshape(block_count * WINDOW_SLOTS, model_dim)
    packed_two = project(flat_rows, w_qkv_two).reshape(block_count, WINDOW_SLOTS, 3 * model_dim)
    head_context = attention_core(packed_two, valid_marks.reshape(block_count, WINDOW_SLOTS) > 0.5)
    mixed_rows = residual_add(flat_rows, head_context, w_out_two).reshape(
        block_count, WINDOW_SLOTS, 1, model_dim
    )
    second_pad = lax.all_to_all(mixed_rows, "grp", split_axis=1, concat_axis=2, tiled=True).reshape(
        slots_all, model_dim
    )
    returning = jnp.take(second_pad, arrived_slot, axis=0, mode="fill", fill_value=0)
    returned = lax.all_to_all(returning, "win", split_axis=0, concat_axis=0, tiled=True)
    encoded = jnp.take(returned, send_place, axis=0)
    return encoded.reshape(1, 1, local_points, model_dim)


def solution(mesh):
    return jax.shard_map(
        on_device,
        mesh=mesh,
        in_specs=(
            P("win", "grp", None, None),
            P("win", "grp", None),
            P(),
            P(),
            P(),
            P(),
            P(),
            P(),
            P(),
        ),
        out_specs=P("win", "grp", None, None),
        check_vma=False,
    )
```

profile of v0, /device:TPU:32, one launch (start us, length us, event | category | flops | bytes accessed | tf_op | source)
XLA Modules:
  0.0 210.3 jit_solution(3294899480315234753)
XLA Ops:
  0.0 0.8 dynamic-slice_bitcast_fusion
  1.6 0.7 add_select_fusion.1
  2.3 0.7 add_select_fusion
  3.1 1.2 reduce-window.6
  4.6 0.7 compare_select_fusion.2
  5.5 0.7 add_subtract_fusion
  6.2 2.4 %scatter_custom_fusion = s32[1024]{0:T(1024)S(1)} fusion(s32[512]{0:T(512)S(1)} %bitcast.161, s32[512]{0:T(512)S(1)} %add_subtract_fusion, s32[]{:T(128)} %constant.120.clone.1), kind=kCustom, calls=%fused_computation.140 | custom fusion | bytes 4100 | tf_op jit(solution)/shard_map/scatter | solution.py:94
  8.7 0.7 all_to_all.49
  9.4 11.4 %all-to-all-start = ((s32[32,32,1]{1,2,0:T(1,128)}), s32[32,32,1]{1,2,0:T(1,128)S(1)}, u32[]{:S(2)}, u32[]{:S(2)}) async-start(s32[32,32,1]{1,2,0:T(1,128)} %all_to_all.49), calls=%async_computation | async-start | bytes 32768 | tf_op jit(solution)/shard_map/all_to_all | solution.py:98
  20.7 4.0 %scatter_custom_fusion.1 = bf16[1024,512]{1,0:T(8,128)(2,1)} fusion(s32[512]{0:T(512)S(1)} %bitcast.162, bf16[1,1,512,512]{3,2,1,0:T(8,128)(2,1)} %param.9, bf16[]{:T(256)} %constant.126.clone.1), kind=kCustom, calls=%fused_computation.82 | custom fusion | bytes 1572866 | tf_op jit(solution)/shard_map/scatter | solution.py:91
  24.7 4.6 %all-to-all-done = s32[32,32,1]{1,2,0:T(1,128)S(1)} async-done(((s32[32,32,1]{1,2,0:T(1,128)}), s32[32,32,1]{1,2,0:T(1,128)S(1)}, u32[]{:S(2)}, u32[]{:S(2)}) %all-to-all-start) | async-done | bytes 4128 | tf_op jit(solution)/shard_map/all_to_all | solution.py:98
  29.3 5.2 %all-to-all-start.1 = ((bf16[32,32,512]{2,1,0:T(8,128)(2,1)}), bf16[32,32,512]{2,1,0:T(8,128)(2,1)S(1)}, u32[]{:S(2)}, u32[]{:S(2)}) async-start(bf16[32,32,512]{2,1,0:T(8,128)(2,1)} %bitcast.12), calls=%async_computation.1 | async-start | bytes 2097152 | tf_op jit(solution)/shard_map/all_to_all | solution.py:97
  34.5 0.9 dynamic-slice_reduce_fusion
  36.7 0.7 reduce.9
  37.6 24.9 %all-to-all-done.1 = bf16[32,32,512]{2,1,0:T(8,128)(2,1)S(1)} async-done(((bf16[32,32,512]{2,1,0:T(8,128)(2,1)}), bf16[32,32,512]{2,1,0:T(8,128)(2,1)S(1)}, u32[]{:S(2)}, u32[]{:S(2)}) %all-to-all-start.1) | async-done | bytes 1048608 | tf_op jit(solution)/shard_map/all_to_all | solution.py:97
  62.5 4.3 %all-to-all-start.3 = ((bf16[8,16,8]{1,0,2:T(8,128)(2,1)}), bf16[8,16,8]{1,0,2:T(8,128)(2,1)S(1)}, u32[]{:S(2)}, u32[]{:S(2)}) async-start(bf16[8,16,8]{1,0,2:T(8,128)(2,1)} %compare_convert_fusion), calls=%async_computation.3 | async-start | bytes 32768 | tf_op jit(solution)/shard_map/all_to_all | solution.py:117
  66.8 5.8 %scatter_custom_fusion.2 = bf16[1024,512]{1,0:T(8,128)(2,1)S(1)} fusion(s32[1024]{0:T(1024)S(1)} %bitcast.159, bf16[1024,512]{1,0:T(8,128)(2,1)} %bitcast.151, bf16[]{:T(256)} %constant.126.clone.1), kind=kCustom, calls=%fused_computation.84 | custom fusion | bytes 1049088 | tf_op jit(solution)/shard_map/scatter | solution.py:104
  73.4 4.9 %convolution_convert_fusion.1 = bf16[1024,1536]{1,0:T(8,128)(2,1)} fusion(bf16[512,1536]{1,0:T(8,128)(2,1)} %param.12, bf16[1024,512]{1,0:T(8,128)(2,1)S(1)} %scatter_custom_fusion.2, f32[1024]{0:T(1024)S(1)} %add_rsqrt_fusion.1, f32[1024]{0:T(1024)S(1)} %broadcast_multiply_fusion.1), kind=kOutput, calls=%fused_computation.34 | convolution fusion | flops 1614282752 | bytes 5775360 | tf_op jit(solution)/shard_map/dot_general | solution.py:20
  78.3 4.7 %copy.120 = bf16[1024,1536]{0,1:T(8,128)(2,1)} copy(bf16[1024,1536]{1,0:T(8,128)(2,1)} %convolution_convert_fusion.1) | data formatting | bytes 6291456 | tf_op jit(solution)/shard_map/convert_element_type | solution.py:20
  83.0 2.7 %copy.155 = bf16[192,8,8,128]{3,2,1,0:T(8,128)(2,1)S(1)} copy(bf16[192,8,8,128]{3,1,2,0:T(8,128)(2,1)} %bitcast.145) | data formatting | bytes 6291456
  86.1 1.3 fusion.52
  87.4 3.5 %fusion.86 = (f32[8,16,128]{2,1,0:T(8,128)S(1)}, f32[8,16,128,128]{2,3,1,0:T(8,128)S(1)}) fusion(f32[8,16,128,128]{2,3,1,0:T(8,128)S(1)} %fusion.52, pred[8,128]{1,0:T(8,128)(4,1)S(1)} %iota_compare_fusion.3), kind=kOutput, calls=%fused_computation.158 | output fusion | flops 12583039 | bytes 16843776 | tf_op jit(solution)/shard_map/sub | solution.py:38
  90.9 1.2 fusion.41
  92.1 0.7 copy.125
  92.8 0.8 convert_reduce_fusion
  93.6 1.0 copy-done.3
  95.1 7.0 %fusion.31 = bf16[1024,512]{1,0:T(8,128)(2,1)S(1)} fusion(bf16[1024,512]{1,0:T(8,128)(2,1)} %copy-done.3, bf16[2048,512]{1,0:T(8,128)(2,1)S(1)} %copy-done, bf16[512,2048]{1,0:T(8,128)(2,1)} %param.14, f32[1024]{0:T(1024)S(1)} %add_rsqrt_fusion, f32[1024]{0:T(1024)S(1)} %broadcast_multiply_fusion), kind=kOutput, calls=%fused_computation.50 | convolution fusion | flops 4317511680 | bytes 6299648 | tf_op jit(solution)/shard_map/dot_general | solution.py:57
  102.2 1.3 copy.126
  103.5 4.8 %all-to-all-start.2 = ((bf16[8,16,8,512]{3,1,0,2:T(8,128)(2,1)}), bf16[8,16,8,512]{3,1,0,2:T(8,128)(2,1)S(1)}, u32[]{:S(2)}, u32[]{:S(2)}) async-start(bf16[8,16,8,512]{3,1,0,2:T(8,128)(2,1)} %copy.126), calls=%async_computation.2 | async-start | bytes 2097152 | tf_op jit(solution)/shard_map/all_to_all | solution.py:110
  108.4 15.8 %all-to-all-done.2 = bf16[8,16,8,512]{3,1,0,2:T(8,128)(2,1)S(1)} async-done(((bf16[8,16,8,512]{3,1,0,2:T(8,128)(2,1)}), bf16[8,16,8,512]{3,1,0,2:T(8,128)(2,1)S(1)}, u32[]{:S(2)}, u32[]{:S(2)}) %all-to-all-start.2) | async-done | bytes 1048608 | tf_op jit(solution)/shard_map/all_to_all | solution.py:110
  126.1 0.8 copy-done.5
  126.9 3.5 %convolution_convert_fusion = bf16[1024,1536]{1,0:T(8,128)(2,1)} fusion(bf16[1024,512]{1,0:T(8,128)(2,1)S(1)} %fusion.33, bf16[512,1536]{1,0:T(8,128)(2,1)S(1)} %copy-done.5), kind=kOutput, calls=%fused_computation.33 | convolution fusion | flops 1612185600 | bytes 5767168 | tf_op jit(solution)/shard_map/dot_general | solution.py:20
  130.3 4.7 %copy.133 = bf16[1024,1536]{0,1:T(8,128)(2,1)} copy(bf16[1024,1536]{1,0:T(8,128)(2,1)} %convolution_convert_fusion) | data formatting | bytes 6291456 | tf_op jit(solution)/shard_map/convert_element_type | solution.py:20
  135.0 2.7 %copy.157 = bf16[192,8,8,128]{3,2,1,0:T(8,128)(2,1)S(1)} copy(bf16[192,8,8,128]{3,1,2,0:T(8,128)(2,1)} %bitcast.146) | data formatting | bytes 6291456
  138.1 1.3 fusion.51
  139.4 3.5 %fusion.87 = (f32[8,16,128]{2,1,0:T(8,128)S(1)}, f32[8,16,128,128]{2,3,1,0:T(8,128)S(1)}) fusion(f32[8,16,128,128]{2,3,1,0:T(8,128)S(1)} %fusion.51, pred[8,128]{1,0:T(8,128)(4,1)S(1)} %gt.23), kind=kOutput, calls=%fused_computation.159 | output fusion | flops 12583039 | bytes 16843776 | tf_op jit(solution)/shard_map/sub | solution.py:38
  142.9 1.2 fusion.42
  144.1 0.7 copy.139
  144.8 0.7 fusion.34
  145.5 1.6 copy.140
  147.1 3.6 %all-to-all-start.4 = ((bf16[8,128,1,512]{3,0,2,1:T(8,128)(2,1)}), bf16[8,128,1,512]{3,0,2,1:T(8,128)(2,1)S(1)}, u32[]{:S(2)}, u32[]{:S(2)}) async-start(bf16[8,128,1,512]{3,0,2,1:T(8,128)(2,1)} %copy.140), calls=%async_computation.4 | async-start | bytes 2097152 | tf_op jit(solution)/shard_map/all_to_all | solution.py:125
  150.7 15.8 %all-to-all-done.4 = bf16[8,128,1,512]{3,0,2,1:T(8,128)(2,1)S(1)} async-done(((bf16[8,128,1,512]{3,0,2,1:T(8,128)(2,1)}), bf16[8,128,1,512]{3,0,2,1:T(8,128)(2,1)S(1)}, u32[]{:S(2)}, u32[]{:S(2)}) %all-to-all-start.4) | async-done | bytes 1048608 | tf_op jit(solution)/shard_map/all_to_all | solution.py:125
  167.1 4.0 %gather_fusion = bf16[1024,512]{1,0:T(8,128)(2,1)S(1)} fusion(bf16[1024,512]{1,0:T(8,128)(2,1)S(1)} %bitcast.141, s32[1024]{0:T(1024)S(1)} %broadcast_clamp_fusion), kind=kCustom, calls=%fused_computation | custom fusion | bytes 2101248 | tf_op jit(solution)/shard_map/jit(_take)/gather | solution.py:128
  171.1 1.2 broadcast_select_fusion
  172.3 5.2 %all-to-all-start.5 = ((bf16[32,32,512]{2,1,0:T(8,128)(2,1)}), bf16[32,32,512]{2,1,0:T(8,128)(2,1)S(1)}, u32[]{:S(2)}, u32[]{:S(2)}) async-start(bf16[32,32,512]{2,1,0:T(8,128)(2,1)} %broadcast_select_fusion), calls=%async_computation.5 | async-start | bytes 2097152 | tf_op jit(solution)/shard_map/all_to_all | solution.py:129
  177.5 28.2 %all-to-all-done.5 = bf16[32,32,512]{2,1,0:T(8,128)(2,1)S(1)} async-done(((bf16[32,32,512]{2,1,0:T(8,128)(2,1)}), bf16[32,32,512]{2,1,0:T(8,128)(2,1)S(1)}, u32[]{:S(2)}, u32[]{:S(2)}) %all-to-all-start.5) | async-done | bytes 1048608 | tf_op jit(solution)/shard_map/all_to_all | solution.py:129
  205.7 2.6 %gather_fusion.1 = bf16[512,512]{1,0:T(8,128)(2,1)} fusion(bf16[1024,512]{1,0:T(8,128)(2,1)S(1)} %bitcast.142, s32[1024]{0:T(1024)S(1)} %pad_clamp_fusion), kind=kCustom, calls=%fused_computation.1 | custom fusion | bytes 1050624 | tf_op jit(solution)/shard_map/jit(_take)/gather | solution.py:130
  208.3 2.0 bitcast_select_fusion
  (59 shorter events, 7.4 us)
Async XLA Ops:
  0.0 95.1 %copy-start = (bf16[2048,512]{1,0:T(8,128)(2,1)S(1)}, bf16[2048,512]{1,0:T(8,128)(2,1)}, u32[]{:S(2)}) copy-start(bf16[2048,512]{1,0:T(8,128)(2,1)} %param.15) | copy-start | bytes 6291460
  9.4 19.9 %all-to-all-start = ((s32[32,32,1]{1,2,0:T(1,128)}), s32[32,32,1]{1,2,0:T(1,128)S(1)}, u32[]{:S(2)}, u32[]{:S(2)}) async-start(s32[32,32,1]{1,2,0:T(1,128)} %all_to_all.49), calls=%async_computation | async-start | bytes 32768 | tf_op jit(solution)/shard_map/all_to_all | solution.py:98
  29.3 33.2 %all-to-all-start.1 = ((bf16[32,32,512]{2,1,0:T(8,128)(2,1)}), bf16[32,32,512]{2,1,0:T(8,128)(2,1)S(1)}, u32[]{:S(2)}, u32[]{:S(2)}) async-start(bf16[32,32,512]{2,1,0:T(8,128)(2,1)} %bitcast.12), calls=%async_computation.1 | async-start | bytes 2097152 | tf_op jit(solution)/shard_map/all_to_all | solution.py:97
  62.5 4.3 %copy-start.2 = (bf16[32,32,512]{2,1,0:T(8,128)(2,1)}, bf16[32,32,512]{2,1,0:T(8,128)(2,1)S(1)}, u32[]{:S(2)}) copy-start(bf16[32,32,512]{2,1,0:T(8,128)(2,1)S(1)} %all-to-all-done.1) | copy-start | bytes 3145732
  62.5 41.0 %all-to-all-start.3 = ((bf16[8,16,8]{1,0,2:T(8,128)(2,1)}), bf16[8,16,8]{1,0,2:T(8,128)(2,1)S(1)}, u32[]{:S(2)}, u32[]{:S(2)}) async-start(bf16[8,16,8]{1,0,2:T(8,128)(2,1)} %compare_convert_fusion), calls=%async_computation.3 | async-start | bytes 32768 | tf_op jit(solution)/shard_map/all_to_all | solution.py:117
  90.8 1.9 copy-start.6
  93.6 1.0 copy-start.3
  103.5 20.7 %all-to-all-start.2 = ((bf16[8,16,8,512]{3,1,0,2:T(8,128)(2,1)}), bf16[8,16,8,512]{3,1,0,2:T(8,128)(2,1)S(1)}, u32[]{:S(2)}, u32[]{:S(2)}) async-start(bf16[8,16,8,512]{3,1,0,2:T(8,128)(2,1)} %copy.126), calls=%async_computation.2 | async-start | bytes 2097152 | tf_op jit(solution)/shard_map/all_to_all | solution.py:110
  125.5 1.4 copy-start.5
  142.9 1.9 copy-start.4
  147.1 19.4 %all-to-all-start.4 = ((bf16[8,128,1,512]{3,0,2,1:T(8,128)(2,1)}), bf16[8,128,1,512]{3,0,2,1:T(8,128)(2,1)S(1)}, u32[]{:S(2)}, u32[]{:S(2)}) async-start(bf16[8,128,1,512]{3,0,2,1:T(8,128)(2,1)} %copy.140), calls=%async_computation.4 | async-start | bytes 2097152 | tf_op jit(solution)/shard_map/all_to_all | solution.py:125
  172.3 33.4 %all-to-all-start.5 = ((bf16[32,32,512]{2,1,0:T(8,128)(2,1)}), bf16[32,32,512]{2,1,0:T(8,128)(2,1)S(1)}, u32[]{:S(2)}, u32[]{:S(2)}) async-start(bf16[32,32,512]{2,1,0:T(8,128)(2,1)} %broadcast_select_fusion), calls=%async_computation.5 | async-start | bytes 2097152 | tf_op jit(solution)/shard_map/all_to_all | solution.py:129
  177.5 32.8 %copy-start.1 = (bf16[2048,512]{1,0:T(8,128)(2,1)S(1)}, bf16[2048,512]{1,0:T(8,128)(2,1)}, u32[]{:S(2)}) copy-start(bf16[2048,512]{1,0:T(8,128)(2,1)} %param.15) | copy-start | bytes 6291460
where the time goes:
time: 211 us; the launch traced here: 210 us
  waiting for transfers between devices  89.3 us (42%)
  local copies, waits for them, and re-layouts  44.9 us (21%)
  starting transfers between devices  34.4 us (16%)
  matrix products  22 us (10%)
  other arithmetic  19.3 us (9%)
    all_to_all x1, waiting for transfers between devices, on_device(): lax.all_to_all(returning, 'win', split_axis=0, concat_axis=0, tiled=True)  28.2 us
    all_to_all x1, waiting for transfers between devices, on_device(): lax.all_to_all(outgoing, 'win', split_axis=0, concat_axis=0, tiled=True)  24.9 us
    all_to_all x1, waiting for transfers between devices, on_device(): lax.all_to_all(mixed_rows, 'grp', split_axis=1, concat_axis=2, tiled=True)  15.8 us
    all_to_all x1, waiting for transfers between devices, on_device(): lax.all_to_all(first_pad.reshape(blocks, dilation_stride, group_count, mo...  15.8 us
    all_to_all x1, starting transfers between devices, on_device(): lax.all_to_all(outgoing_slot, 'win', split_axis=0, concat_axis=0, tiled=T...  11.4 us
    convert_element_type x2, local copies, waits for them, and re-layouts, project(): jnp.dot(normalize(row_data), weight, preferred_element_type=jnp.float32)  9.38 us
    dot_general x2, matrix products, project(): jnp.dot(normalize(row_data), weight, preferred_element_type=jnp.float32)  8.39 us
    unnamed x16, local copies, waits for them, and re-layouts  7.21 us
  transfers between devices with their start and end apart: 6, of which 5 were waited for; matrix products, arithmetic and copies ran while one was open for 20% of the time, Pallas kernels for 0%

commit v1 on v0

--- a/solution.py
+++ b/solution.py
@@ -1,3 +1,4 @@
+import functools
 import jax
 import jax.numpy as jnp
 from jax import lax
@@ -7,6 +8,22 @@
 WINDOW_SLOTS = 128
 EPSILON = 1e-05
 MASKED = -1e30
+
+
+def _build_masks(sheet, dim_no, d0):
+    z = jnp.concatenate(
+        lax.all_to_all(
+            jnp.stack(jnp.split(sheet, lax.axis_size("grp"), axis=dim_no), axis=0),
+            "grp",
+            split_axis=0,
+            concat_axis=0,
+        ),
+        axis=d0,
+    )
+    return z
+
+
+_draw_gates = functools.partial(_build_masks, dim_no=1, d0=2)
 
 
 def normalize(row_data):
@@ -122,9 +139,7 @@
     mixed_rows = residual_add(flat_rows, head_context, w_out_two).reshape(
         block_count, WINDOW_SLOTS, 1, model_dim
     )
-    second_pad = lax.all_to_all(mixed_rows, "grp", split_axis=1, concat_axis=2, tiled=True).reshape(
-        slots_all, model_dim
-    )
+    second_pad = _draw_gates(mixed_rows).reshape(slots_all, model_dim)
     returning = jnp.take(second_pad, arrived_slot, axis=0, mode="fill", fill_value=0)
     returned = lax.all_to_all(returning, "win", split_axis=0, concat_axis=0, tiled=True)
     encoded = jnp.take(returned, send_place, axis=0)

time: 211 us -> 215 us (1.019)
  local copies, waits for them, and re-layouts: 44.9 us -> 48.7 us
    unnamed x16 -> x23, local copies, waits for them, and re-layouts: 7.21 us -> 11.8 us
where the time goes in v1:
time: 215 us; the launch traced here: 214 us
  waiting for transfers between devices  89.3 us (42%)
  local copies, waits for them, and re-layouts  48.7 us (23%)
  starting transfers between devices  34.4 us (16%)
  matrix products  22 us (10%)
  other arithmetic  19.3 us (9%)
    all_to_all x1, waiting for transfers between devices, on_device(): lax.all_to_all(returning, 'win', split_axis=0, concat_axis=0, tiled=True)  28.2 us
    all_to_all x1, waiting for transfers between devices, on_device(): lax.all_to_all(outgoing, 'win', split_axis=0, concat_axis=0, tiled=True)  24.9 us
    all_to_all x1, waiting for transfers between devices, _build_masks(): lax.all_to_all(jnp.stack(jnp.split(sheet, lax.axis_size('grp'), axis=dim_...  15.8 us
    all_to_all x1, waiting for transfers between devices, on_device(): lax.all_to_all(first_pad.reshape(blocks, dilation_stride, group_count, mo...  15.8 us
    unnamed x23, local copies, waits for them, and re-layouts  11.8 us
    all_to_all x1, starting transfers between devices, on_device(): lax.all_to_all(outgoing_slot, 'win', split_axis=0, concat_axis=0, tiled=T...  11.4 us
    convert_element_type x2, local copies, waits for them, and re-layouts, project(): jnp.dot(normalize(row_data), weight, preferred_element_type=jnp.float32)  9.38 us
    dot_general x2, matrix products, project(): jnp.dot(normalize(row_data), weight, preferred_element_type=jnp.float32)  8.39 us
  transfers between devices with their start and end apart: 6, of which 5 were waited for; matrix products, arithmetic and copies ran while one was open for 20% of the time, Pallas kernels for 0%

profile of v1, /device:TPU:32, one launch (start us, length us, event | category | flops | bytes accessed | tf_op | source)
XLA Modules:
  0.0 214.1 jit_solution(17143753783236605721)
XLA Ops:
  0.0 0.8 dynamic-slice_bitcast_fusion
  0.9 0.7 fusion.78
  1.6 0.7 add_select_fusion.1
  2.3 0.7 add_select_fusion
  3.1 1.2 reduce-window.6
  4.6 0.7 compare_select_fusion.2
  5.5 0.7 add_subtract_fusion
  6.2 2.4 %scatter_custom_fusion = s32[1024]{0:T(1024)S(1)} fusion(s32[512]{0:T(512)S(1)} %bitcast.198, s32[512]{0:T(512)S(1)} %add_subtract_fusion, s32[]{:T(128)} %constant.120.clone.1), kind=kCustom, calls=%fused_computation.156 | custom fusion | bytes 4100 | tf_op jit(solution)/shard_map/scatter | solution.py:111
  8.7 0.7 all_to_all.41
  9.4 11.4 %all-to-all-start = ((s32[32,32,1]{1,2,0:T(1,128)}), s32[32,32,1]{1,2,0:T(1,128)S(1)}, u32[]{:S(2)}, u32[]{:S(2)}) async-start(s32[32,32,1]{1,2,0:T(1,128)} %all_to_all.41), calls=%async_computation | async-start | bytes 32768 | tf_op jit(solution)/shard_map/all_to_all | solution.py:115
  20.7 4.0 %scatter_custom_fusion.1 = bf16[1024,512]{1,0:T(8,128)(2,1)} fusion(s32[512]{0:T(512)S(1)} %bitcast.199, bf16[1,1,512,512]{3,2,1,0:T(8,128)(2,1)} %param.9, bf16[]{:T(256)} %constant.126.clone.1), kind=kCustom, calls=%fused_computation.82 | custom fusion | bytes 1572866 | tf_op jit(solution)/shard_map/scatter | solution.py:108
  24.7 4.6 %all-to-all-done = s32[32,32,1]{1,2,0:T(1,128)S(1)} async-done(((s32[32,32,1]{1,2,0:T(1,128)}), s32[32,32,1]{1,2,0:T(1,128)S(1)}, u32[]{:S(2)}, u32[]{:S(2)}) %all-to-all-start) | async-done | bytes 4128 | tf_op jit(solution)/shard_map/all_to_all | solution.py:115
  29.3 5.2 %all-to-all-start.1 = ((bf16[32,32,512]{2,1,0:T(8,128)(2,1)}), bf16[32,32,512]{2,1,0:T(8,128)(2,1)S(1)}, u32[]{:S(2)}, u32[]{:S(2)}) async-start(bf16[32,32,512]{2,1,0:T(8,128)(2,1)} %bitcast.12), calls=%async_computation.1 | async-start | bytes 2097152 | tf_op jit(solution)/shard_map/all_to_all | solution.py:114
  34.5 0.9 dynamic-slice_reduce_fusion
  36.7 0.7 reduce.9
  37.6 24.9 %all-to-all-done.1 = bf16[32,32,512]{2,1,0:T(8,128)(2,1)S(1)} async-done(((bf16[32,32,512]{2,1,0:T(8,128)(2,1)}), bf16[32,32,512]{2,1,0:T(8,128)(2,1)S(1)}, u32[]{:S(2)}, u32[]{:S(2)}) %all-to-all-start.1) | async-done | bytes 1048608 | tf_op jit(solution)/shard_map/all_to_all | solution.py:114
  62.5 4.3 %all-to-all-start.3 = ((bf16[8,16,8]{1,0,2:T(8,128)(2,1)}), bf16[8,16,8]{1,0,2:T(8,128)(2,1)S(1)}, u32[]{:S(2)}, u32[]{:S(2)}) async-start(bf16[8,16,8]{1,0,2:T(8,128)(2,1)} %compare_convert_fusion), calls=%async_computation.3 | async-start | bytes 32768 | tf_op jit(solution)/shard_map/all_to_all | solution.py:134
  66.8 5.8 %scatter_custom_fusion.2 = bf16[1024,512]{1,0:T(8,128)(2,1)S(1)} fusion(s32[1024]{0:T(1024)S(1)} %bitcast.196, bf16[1024,512]{1,0:T(8,128)(2,1)} %bitcast.188, bf16[]{:T(256)} %constant.126.clone.1), kind=kCustom, calls=%fused_computation.84 | custom fusion | bytes 1049088 | tf_op jit(solution)/shard_map/scatter | solution.py:121
  73.4 4.9 %convolution_convert_fusion.1 = bf16[1024,1536]{1,0:T(8,128)(2,1)} fusion(bf16[512,1536]{1,0:T(8,128)(2,1)} %param.12, bf16[1024,512]{1,0:T(8,128)(2,1)S(1)} %scatter_custom_fusion.2, f32[1024]{0:T(1024)S(1)} %add_rsqrt_fusion.1, f32[1024]{0:T(1024)S(1)} %broadcast_multiply_fusion.1), kind=kOutput, calls=%fused_computation.34 | convolution fusion | flops 1614282752 | bytes 5775360 | tf_op jit(solution)/shard_map/dot_general | solution.py:37
  78.3 4.7 %copy.117 = bf16[1024,1536]{0,1:T(8,128)(2,1)} copy(bf16[1024,1536]{1,0:T(8,128)(2,1)} %convolution_convert_fusion.1) | data formatting | bytes 6291456 | tf_op jit(solution)/shard_map/convert_element_type | solution.py:37
  83.0 2.7 %copy.151 = bf16[192,8,8,128]{3,2,1,0:T(8,128)(2,1)S(1)} copy(bf16[192,8,8,128]{3,1,2,0:T(8,128)(2,1)} %bitcast.175) | data formatting | bytes 6291456
  86.1 1.3 fusion.52
  87.4 3.5 %fusion.94 = (f32[8,16,128]{2,1,0:T(8,128)S(1)}, f32[8,16,128,128]{2,3,1,0:T(8,128)S(1)}) fusion(f32[8,16,128,128]{2,3,1,0:T(8,128)S(1)} %fusion.52, pred[8,128]{1,0:T(8,128)(4,1)S(1)} %iota_compare_fusion.3), kind=kOutput, calls=%fused_computation.174 | output fusion | flops 12583039 | bytes 16843776 | tf_op jit(solution)/shard_map/sub | solution.py:55
  90.9 1.2 fusion.41
  92.1 0.7 copy.122
  92.8 0.8 convert_reduce_fusion
  93.6 1.0 copy-done.3
  95.1 7.0 %fusion.31 = bf16[1024,512]{1,0:T(8,128)(2,1)S(1)} fusion(bf16[1024,512]{1,0:T(8,128)(2,1)} %copy-done.3, bf16[2048,512]{1,0:T(8,128)(2,1)S(1)} %copy-done, bf16[512,2048]{1,0:T(8,128)(2,1)} %param.14, f32[1024]{0:T(1024)S(1)} %add_rsqrt_fusion, f32[1024]{0:T(1024)S(1)} %broadcast_multiply_fusion), kind=kOutput, calls=%fused_computation.50 | convolution fusion | flops 4317511680 | bytes 6299648 | tf_op jit(solution)/shard_map/dot_general | solution.py:74
  102.2 1.3 copy.123
  103.5 4.8 %all-to-all-start.2 = ((bf16[8,16,8,512]{3,1,0,2:T(8,128)(2,1)}), bf16[8,16,8,512]{3,1,0,2:T(8,128)(2,1)S(1)}, u32[]{:S(2)}, u32[]{:S(2)}) async-start(bf16[8,16,8,512]{3,1,0,2:T(8,128)(2,1)} %copy.123), calls=%async_computation.2 | async-start | bytes 2097152 | tf_op jit(solution)/shard_map/all_to_all | solution.py:127
  108.4 15.8 %all-to-all-done.2 = bf16[8,16,8,512]{3,1,0,2:T(8,128)(2,1)S(1)} async-done(((bf16[8,16,8,512]{3,1,0,2:T(8,128)(2,1)}), bf16[8,16,8,512]{3,1,0,2:T(8,128)(2,1)S(1)}, u32[]{:S(2)}, u32[]{:S(2)}) %all-to-all-start.2) | async-done | bytes 1048608 | tf_op jit(solution)/shard_map/all_to_all | solution.py:127
  126.1 0.8 copy-done.5
  126.9 3.5 %convolution_convert_fusion = bf16[1024,1536]{1,0:T(8,128)(2,1)} fusion(bf16[1024,512]{1,0:T(8,128)(2,1)S(1)} %fusion.33, bf16[512,1536]{1,0:T(8,128)(2,1)S(1)} %copy-done.5), kind=kOutput, calls=%fused_computation.33 | convolution fusion | flops 1612185600 | bytes 5767168 | tf_op jit(solution)/shard_map/dot_general | solution.py:37
  130.3 4.7 %copy.130 = bf16[1024,1536]{0,1:T(8,128)(2,1)} copy(bf16[1024,1536]{1,0:T(8,128)(2,1)} %convolution_convert_fusion) | data formatting | bytes 6291456 | tf_op jit(solution)/shard_map/convert_element_type | solution.py:37
  135.0 2.7 %copy.153 = bf16[192,8,8,128]{3,2,1,0:T(8,128)(2,1)S(1)} copy(bf16[192,8,8,128]{3,1,2,0:T(8,128)(2,1)} %bitcast.176) | data formatting | bytes 6291456
  138.1 1.3 fusion.51
  139.4 3.5 %fusion.95 = (f32[8,16,128]{2,1,0:T(8,128)S(1)}, f32[8,16,128,128]{2,3,1,0:T(8,128)S(1)}) fusion(f32[8,16,128,128]{2,3,1,0:T(8,128)S(1)} %fusion.51, pred[8,128]{1,0:T(8,128)(4,1)S(1)} %gt.23), kind=kOutput, calls=%fused_computation.175 | output fusion | flops 12583039 | bytes 16843776 | tf_op jit(solution)/shard_map/sub | solution.py:55
  142.9 1.2 fusion.42
  144.1 0.7 copy.136
  144.8 0.7 fusion.34
  150.8 3.6 %all-to-all-start.4 = ((bf16[8,8,16,1,512]{4,2,1,3,0:T(8,128)(2,1)}), bf16[8,8,16,1,512]{4,2,1,3,0:T(8,128)(2,1)S(1)}, u32[]{:S(2)}, u32[]{:S(2)}) async-start(bf16[8,8,16,1,512]{4,2,1,3,0:T(8,128)(2,1)} %fusion.64), calls=%async_computation.4 | async-start | bytes 2097152 | tf_op jit(solution)/shard_map/all_to_all | solution.py:15
  154.4 15.8 %all-to-all-done.4 = bf16[8,8,16,1,512]{4,2,1,3,0:T(8,128)(2,1)S(1)} async-done(((bf16[8,8,16,1,512]{4,2,1,3,0:T(8,128)(2,1)}), bf16[8,8,16,1,512]{4,2,1,3,0:T(8,128)(2,1)S(1)}, u32[]{:S(2)}, u32[]{:S(2)}) %all-to-all-start.4) | async-done | bytes 1048608 | tf_op jit(solution)/shard_map/all_to_all | solution.py:15
  170.8 4.0 %gather_fusion = bf16[1024,512]{1,0:T(8,128)(2,1)S(1)} fusion(bf16[1024,512]{1,0:T(8,128)(2,1)S(1)} %bitcast.171, s32[1024]{0:T(1024)S(1)} %broadcast_clamp_fusion), kind=kCustom, calls=%fused_computation | custom fusion | bytes 2101248 | tf_op jit(solution)/shard_map/jit(_take)/gather | solution.py:143
  174.8 1.2 broadcast_select_fusion
  176.0 5.2 %all-to-all-start.5 = ((bf16[32,32,512]{2,1,0:T(8,128)(2,1)}), bf16[32,32,512]{2,1,0:T(8,128)(2,1)S(1)}, u32[]{:S(2)}, u32[]{:S(2)}) async-start(bf16[32,32,512]{2,1,0:T(8,128)(2,1)} %broadcast_select_fusion), calls=%async_computation.5 | async-start | bytes 2097152 | tf_op jit(solution)/shard_map/all_to_all | solution.py:144
  181.3 28.2 %all-to-all-done.5 = bf16[32,32,512]{2,1,0:T(8,128)(2,1)S(1)} async-done(((bf16[32,32,512]{2,1,0:T(8,128)(2,1)}), bf16[32,32,512]{2,1,0:T(8,128)(2,1)S(1)}, u32[]{:S(2)}, u32[]{:S(2)}) %all-to-all-start.5) | async-done | bytes 1048608 | tf_op jit(solution)/shard_map/all_to_all | solution.py:144
  209.5 2.6 %gather_fusion.1 = bf16[512,512]{1,0:T(8,128)(2,1)} fusion(bf16[1024,512]{1,0:T(8,128)(2,1)S(1)} %bitcast.172, s32[1024]{0:T(1024)S(1)} %pad_clamp_fusion), kind=kCustom, calls=%fused_computation.1 | custom fusion | bytes 1050624 | tf_op jit(solution)/shard_map/jit(_take)/gather | solution.py:145
  212.1 2.0 bitcast_select_fusion
  (66 shorter events, 12.0 us)
Async XLA Ops:
  0.0 95.1 %copy-start = (bf16[2048,512]{1,0:T(8,128)(2,1)S(1)}, bf16[2048,512]{1,0:T(8,128)(2,1)}, u32[]{:S(2)}) copy-start(bf16[2048,512]{1,0:T(8,128)(2,1)} %param.15) | copy-start | bytes 6291460
  9.4 19.9 %all-to-all-start = ((s32[32,32,1]{1,2,0:T(1,128)}), s32[32,32,1]{1,2,0:T(1,128)S(1)}, u32[]{:S(2)}, u32[]{:S(2)}) async-start(s32[32,32,1]{1,2,0:T(1,128)} %all_to_all.41), calls=%async_computation | async-start | bytes 32768 | tf_op jit(solution)/shard_map/all_to_all | solution.py:115
  29.3 33.2 %all-to-all-start.1 = ((bf16[32,32,512]{2,1,0:T(8,128)(2,1)}), bf16[32,32,512]{2,1,0:T(8,128)(2,1)S(1)}, u32[]{:S(2)}, u32[]{:S(2)}) async-start(bf16[32,32,512]{2,1,0:T(8,128)(2,1)} %bitcast.12), calls=%async_computation.1 | async-start | bytes 2097152 | tf_op jit(solution)/shard_map/all_to_all | solution.py:114
  62.5 4.3 %copy-start.2 = (bf16[32,32,512]{2,1,0:T(8,128)(2,1)}, bf16[32,32,512]{2,1,0:T(8,128)(2,1)S(1)}, u32[]{:S(2)}) copy-start(bf16[32,32,512]{2,1,0:T(8,128)(2,1)S(1)} %all-to-all-done.1) | copy-start | bytes 3145732
  62.5 41.0 %all-to-all-start.3 = ((bf16[8,16,8]{1,0,2:T(8,128)(2,1)}), bf16[8,16,8]{1,0,2:T(8,128)(2,1)S(1)}, u32[]{:S(2)}, u32[]{:S(2)}) async-start(bf16[8,16,8]{1,0,2:T(8,128)(2,1)} %compare_convert_fusion), calls=%async_computation.3 | async-start | bytes 32768 | tf_op jit(solution)/shard_map/all_to_all | solution.py:134
  90.8 1.9 copy-start.6
  93.6 1.0 copy-start.3
  103.5 20.7 %all-to-all-start.2 = ((bf16[8,16,8,512]{3,1,0,2:T(8,128)(2,1)}), bf16[8,16,8,512]{3,1,0,2:T(8,128)(2,1)S(1)}, u32[]{:S(2)}, u32[]{:S(2)}) async-start(bf16[8,16,8,512]{3,1,0,2:T(8,128)(2,1)} %copy.123), calls=%async_computation.2 | async-start | bytes 2097152 | tf_op jit(solution)/shard_map/all_to_all | solution.py:127
  125.5 1.4 copy-start.5
  142.9 1.9 copy-start.4
  150.8 19.4 %all-to-all-start.4 = ((bf16[8,8,16,1,512]{4,2,1,3,0:T(8,128)(2,1)}), bf16[8,8,16,1,512]{4,2,1,3,0:T(8,128)(2,1)S(1)}, u32[]{:S(2)}, u32[]{:S(2)}) async-start(bf16[8,8,16,1,512]{4,2,1,3,0:T(8,128)(2,1)} %fusion.64), calls=%async_computation.4 | async-start | bytes 2097152 | tf_op jit(solution)/shard_map/all_to_all | solution.py:15
  176.0 33.4 %all-to-all-start.5 = ((bf16[32,32,512]{2,1,0:T(8,128)(2,1)}), bf16[32,32,512]{2,1,0:T(8,128)(2,1)S(1)}, u32[]{:S(2)}, u32[]{:S(2)}) async-start(bf16[32,32,512]{2,1,0:T(8,128)(2,1)} %broadcast_select_fusion), calls=%async_computation.5 | async-start | bytes 2097152 | tf_op jit(solution)/shard_map/all_to_all | solution.py:144
  181.2 32.8 %copy-start.1 = (bf16[2048,512]{1,0:T(8,128)(2,1)S(1)}, bf16[2048,512]{1,0:T(8,128)(2,1)}, u32[]{:S(2)}) copy-start(bf16[2048,512]{1,0:T(8,128)(2,1)} %param.15) | copy-start | bytes 6291460
